TPU v7x, 128 devices: a whole 4x4x4 slice. The times are simulated.
128 devices in a mesh: dp: 32 (over x_lo, z, y), mp: 4 (over x_hi, core).
Axes of the slice: x: 4 (x_hi: 2, x_lo: 2; x = x_hi * 2 + x_lo), y: 4, z: 4, core: 2. Of those that a mesh axis runs over, the one named last changes fastest.
Arguments:
- samples: bfloat16 [24576, 8192], P('dp', 'mp'), may hold values from -6 to 6
- gain: float32 [8192], P('mp'), may hold values from 0.1 to 1.9
- left_blocks: bfloat16 [64, 128, 128], P('mp'), may hold values from -0.5 to 0.5
- gate_blocks: bfloat16 [64, 128, 128], P('mp'), may hold values from -0.5 to 0.5
- right_blocks: bfloat16 [64, 128, 128], P('mp'), may hold values from -0.5 to 0.5
- cotangent: bfloat16 [24576, 8192], P('dp', 'mp'), may hold values from -6 to 6
Outputs:
- grad_input: bfloat16 [24576, 8192], P('dp', 'mp')
- grad_left: float32 [64, 128, 128], P('mp')
- grad_gate: float32 [64, 128, 128], P('mp')
- grad_right: float32 [64, 128, 128], P('mp')
All inputs are finite; a program needn't handle non-finite values.
Results may differ from a plain program's by a relative error of at most 0.007.
Values may be sent and summed in bfloat16 or wider, within the bound.
No kernel may reach another device: no remote copies, remote signals or barrier semaphores. Data moves between devices by JAX's collectives and lax.ppermute only.
A program may use at most 128 MiB of HBM per device.

v0:
```python
import jax
import jax.numpy as jnp
from jax import lax
from jax.sharding import PartitionSpec as P

W = 8192
BLOCK = 128
NBLK = 64


def body(samples, gain, left_blocks, gate_blocks, right_blocks, cotangent):
    rows, width_local = samples.shape
    nlocal = left_blocks.shape[0]
    xf = samples.astype(jnp.float32)
    squares = lax.psum(jnp.sum(xf * xf, axis=1), "mp")
    rstd = lax.rsqrt(squares / W + 1e-05)[:, None]
    xn = (xf * rstd * gain).astype(jnp.bfloat16).reshape(rows, nlocal, BLOCK)
    act_a = jnp.einsum("tic,icj->tij", xn, left_blocks, preferred_element_type=jnp.float32)
    act_g = jnp.einsum("tic,icj->tij", xn, gate_blocks, preferred_element_type=jnp.float32)
    silu_g = jax.nn.silu(act_g)
    gated = (act_a * silu_g).astype(jnp.bfloat16)
    outgoing = (
        gated.reshape(rows, nlocal, NBLK, 2).transpose(0, 2, 1, 3).reshape(rows, NBLK, 2 * nlocal)
    )
    cot_blocks = cotangent.reshape(rows, nlocal, BLOCK)
    grad_perm = jnp.einsum(
        "tkm,kcm->tkc", cot_blocks, right_blocks, preferred_element_type=jnp.float32
    ).astype(jnp.bfloat16)
    permuted = lax.all_to_all(outgoing, "mp", split_axis=1, concat_axis=2, tiled=True)
    right_local = jnp.einsum(
        "tkc,tkm->kcm", permuted, cot_blocks, preferred_element_type=jnp.float32
    )
    returned = lax.all_to_all(grad_perm, "mp", split_axis=2, concat_axis=1, tiled=True)
    grad_gated = (
        returned.reshape(rows, NBLK, nlocal, 2)
        .transpose(0, 2, 1, 3)
        .reshape(rows, nlocal, BLOCK)
        .astype(jnp.float32)
    )
    sigma = jax.nn.sigmoid(act_g)
    grad_a = (grad_gated * silu_g).astype(jnp.bfloat16)
    grad_g = (grad_gated * act_a * sigma * (1.0 + act_g * (1.0 - sigma))).astype(jnp.bfloat16)
    left_local = jnp.einsum("tic,tij->icj", xn, grad_a, preferred_element_type=jnp.float32)
    gate_local = jnp.einsum("tic,tij->icj", xn, grad_g, preferred_element_type=jnp.float32)
    grad_norm = jnp.einsum("tij,icj->tic", grad_a, left_blocks, preferred_element_type=jnp.float32)
    grad_norm = grad_norm + jnp.einsum(
        "tij,icj->tic", grad_g, gate_blocks, preferred_element_type=jnp.float32
    )
    scaled = grad_norm.reshape(rows, width_local) * gain
    inner = lax.psum(jnp.sum(scaled * xf, axis=1), "mp")
    mean_inner = (inner / W)[:, None]
    grad_input = (
        cotangent.astype(jnp.float32) + rstd * (scaled - xf * rstd * rstd * mean_inner)
    ).astype(jnp.bfloat16)
    left_total, gate_total, right_total = lax.psum((left_local, gate_local, right_local), "dp")
    return (grad_input, left_total, gate_total, right_total)


def solution(mesh):
    placed = (
        P("dp", "mp"),
        P("mp"),
        P("mp", None, None),
        P("mp", None, None),
        P("mp", None, None),
        P("dp", "mp"),
    )
    return jax.shard_map(
        body,
        mesh=mesh,
        in_specs=placed,
        out_specs=(P("dp", "mp"), P("mp", None, None), P("mp", None, None), P("mp", None, None)),
        check_vma=False,
    )
```

profile of v0, /device:TPU:6, one launch (start us, length us, event | category | flops | bytes accessed | tf_op | source)
XLA Modules:
  0.0 503.4 jit_solution(17954740731904639991)
XLA Ops:
  7.2 3.1 convert_bitcast_fusion.1
  10.3 3.4 copy.60
  13.7 6.0 %all-to-all-start = ((bf16[768,16,128]{0,1,2:T(8,128)(2,1)}), bf16[768,16,128]{0,1,2:T(8,128)(2,1)}, u32[]{:S(2)}, u32[]{:S(2)}) async-start(bf16[768,16,128]{0,1,2:T(8,128)(2,1)} %copy.60), calls=%async_computation | async-start | bytes 6291456 | tf_op jit(solution)/shard_map/all_to_all | solution.py:33
  22.2 37.0 %psum.35 = f32[768]{0:T(1024)S(1)} all-reduce(f32[768]{0:T(1024)S(1)} %fusion.8), channel_id=1, replica_groups=mesh['dp'=32,'mp'=4] {'mp'}, use_global_device_ids=true, to_apply=%region_1.0 | all-reduce | flops 768 | bytes 6144 | tf_op jit(solution)/shard_map/psum | solution.py:15
  59.3 4.3 fusion.2
  63.6 4.7 copy.85
  68.4 5.6 %fusion.26 = f32[16,768,128]{1,2,0:T(8,128)} fusion(bf16[768,16,128]{0,2,1:T(8,128)(2,1)} %bitcast.85, bf16[16,128,128]{2,1,0:T(8,128)(2,1)S(1)} %copy-done.5), kind=kOutput, calls=%fused_computation.38 | convolution fusion | flops 402653184 | bytes 9961472 | tf_op jit(solution)/shard_map/tic,icj->tij/dot_general | solution.py:19
  73.9 2.9 copy.61
  77.7 6.3 %copy.62 = f32[768,4,16,32]{0,2,1,3:T(8,128)} copy(f32[768,4,16,32]{0,3,1,2:T(8,128)S(1)} %convert_bitcast_fusion) | data formatting | bytes 12582912 | tf_op jit(solution)/shard_map/convert_element_type | solution.py:38
  84.0 10.3 %copy.63 = f32[768,16,64,2]{0,3,2,1:T(2,128)} copy(f32[768,16,64,2]{0,2,3,1:T(8,128)} %bitcast.89) | data formatting | bytes 12582912 | tf_op jit(solution)/shard_map/convert_element_type | solution.py:38
  94.3 8.5 %reshape.38 = f32[768,16,128]{0,2,1:T(8,128)} reshape(f32[768,16,64,2]{0,3,2,1:T(2,128)} %copy.63) | data formatting | bytes 12582912 | tf_op jit(solution)/shard_map/convert_element_type | solution.py:38
  102.7 9.7 %fusion.13 = (bf16[768,16,128]{0,2,1:T(8,128)(2,1)}, bf16[768,16,128]{0,2,1:T(8,128)(2,1)}, bf16[768,16,128]{0,2,1:T(8,128)(2,1)}) fusion(f32[16,768,128]{1,2,0:T(8,128)} %fusion.26, f32[768,16,128]{0,2,1:T(8,128)} %reshape.38, bf16[768,16,128]{0,2,1:T(8,128)(2,1)} %bitcast.86, bf16[16,128,128]{2,1,0:T(8,128)(2,1)S(1)} %copy-done), kind=kOutput, calls=%fused_computation.19 | convolution fusion | flops 426246144 | bytes 25690112 | tf_op jit(solution)/shard_map/tic,icj->tij/dot_general | solution.py:18
  112.5 7.3 %reshape.36 = bf16[768,16,64,2]{0,3,2,1:T(2,128)(2,1)} reshape(bf16[768,16,128]{0,2,1:T(8,128)(2,1)} %get-tuple-element.7) | data formatting | bytes 6291456 | tf_op jit(solution)/shard_map/reshape | solution.py:23
  122.3 3.4 copy.76
  125.7 5.0 all-to-all-start.1
  130.7 4.9 fusion.28
  137.6 28.5 %all-to-all-done.1 = bf16[768,64,32]{0,2,1:T(8,128)(2,1)} async-done(((bf16[768,64,32]{0,2,1:T(8,128)(2,1)}), bf16[768,64,32]{0,2,1:T(8,128)(2,1)}, u32[]{:S(2)}, u32[]{:S(2)}) %all-to-all-start.1) | async-done | bytes 3145760 | tf_op jit(solution)/shard_map/all_to_all | solution.py:29
  170.9 3.0 fusion.29
  173.9 3.6 convolution_add_fusion
  177.5 6.6 %copy.70 = f32[768,2048]{1,0:T(8,128)} copy(f32[768,2048]{0,1:T(8,128)} %bitcast.90) | data formatting | bytes 12582912 | tf_op jit(solution)/shard_map/reshape | solution.py:49
  184.1 4.6 fusion.9
  188.7 9.6 %psum.36 = f32[768]{0:T(1024)S(1)} all-reduce(f32[768]{0:T(1024)S(1)} %fusion.9), channel_id=1, replica_groups=mesh['dp'=32,'mp'=4] {'mp'}, use_global_device_ids=true, to_apply=%region_3.4 | all-reduce | flops 768 | bytes 6144 | tf_op jit(solution)/shard_map/psum | solution.py:50
  198.3 6.9 %fusion.7 = bf16[768,2048]{1,0:T(8,128)(2,1)} fusion(bf16[768,2048]{1,0:T(8,128)(2,1)} %param.6, bf16[768,2048]{1,0:T(8,128)(2,1)} %param.11, f32[768,2048]{1,0:T(8,128)} %copy.70, f32[768]{0:T(1024)S(1)} %broadcast_multiply_fusion, f32[2048]{0:T(1024)S(1)} %copy-done.7, f32[768]{0:T(1024)S(1)} %add_rsqrt_fusion), kind=kLoop, calls=%fused_computation.10 | loop fusion | flops 15728640 | bytes 15742976 | tf_op jit(solution)/shard_map/convert_element_type | solution.py:54
  205.3 285.6 %all-reduce.3.cloned.1.call-done = (f32[16,128,128]{2,1,0:T(8,128)}, f32[16,128,128]{2,1,0:T(8,128)}, f32[16,128,128]{2,1,0:T(8,128)}) async-done(((f32[16,128,128]{2,1,0:T(8,128)}, f32[16,128,128]{2,1,0:T(8,128)}, f32[16,128,128]{2,1,0:T(8,128)}), (f32[16,128,128]{2,1,0:T(8,128)}, f32[16,128,128]{2,1,0:T(8,128)}, f32[16,128,128]{2,1,0:T(8,128)})) %all-reduce.3.cloned.1.call-update) | async-done | bytes 3145744 | tf_op jit(solution)/shard_map/psum | solution.py:55
  (30 shorter events, 18.4 us)
Async XLA Ops:
  7.2 95.6 %copy-start = (bf16[16,128,128]{2,1,0:T(8,128)(2,1)S(1)}, bf16[16,128,128]{2,1,0:T(8,128)(2,1)}, u32[]{:S(2)}) copy-start(bf16[16,128,128]{2,1,0:T(8,128)(2,1)} %param.8) | copy-start | bytes 1572868
  13.7 60.3 %all-to-all-start = ((bf16[768,16,128]{0,1,2:T(8,128)(2,1)}), bf16[768,16,128]{0,1,2:T(8,128)(2,1)}, u32[]{:S(2)}, u32[]{:S(2)}) async-start(bf16[768,16,128]{0,1,2:T(8,128)(2,1)} %copy.60), calls=%async_computation | async-start | bytes 6291456 | tf_op jit(solution)/shard_map/all_to_all | solution.py:33
  19.7 39.6 %copy-start.7 = (f32[2048]{0:T(1024)S(1)}, f32[2048]{0:T(1024)}, u32[]{:S(2)}) copy-start(f32[2048]{0:T(1024)} %param.7) | copy-start | bytes 24580
  63.6 4.7 copy-start.5
  125.7 40.3 %all-to-all-start.1 = ((bf16[768,64,32]{0,2,1:T(8,128)(2,1)}), bf16[768,64,32]{0,2,1:T(8,128)(2,1)}, u32[]{:S(2)}, u32[]{:S(2)}) async-start(bf16[768,64,32]{0,2,1:T(8,128)(2,1)} %copy.76), calls=%async_computation.1 | async-start | bytes 6291456 | tf_op jit(solution)/shard_map/all_to_all | solution.py:29
  130.7 360.2 %all-reduce.3.cloned.1.call-start = ((), (), s32[]{:S(2)}) async-start(), calls=%async_computation.2 | async-start | bytes 6291456 | tf_op jit(solution)/shard_map/psum | solution.py:55
  130.7 4.9 copy-start.1
  130.7 4.9 copy-start.2
  166.1 2.8 copy-start.3
  170.9 3.0 copy-start.4
  490.9 4.7 copy-start.6
Sparse Core Ops, SparseCore 0:
  171.0 319.8 all-reduce.2
where the time goes:
time: 505 us; the launch traced here: 503 us
  waiting for transfers between devices  314 us (62%)
  local copies, waits for them, and re-layouts  64.4 us (13%)
  blocking collectives  46.7 us (9%)
  matrix products  33.9 us (7%)
  other arithmetic  19.3 us (4%)
  between operations  14.1 us (3%)
  starting transfers between devices  11 us (2%)
    psum x1, waiting for transfers between devices, body(): lax.psum((left_local, gate_local, right_local), 'dp')  286 us
    psum x1, blocking collectives, body(): squares = lax.psum(jnp.sum(xf * xf, axis=1), 'mp')  37 us
    all_to_all x1, waiting for transfers between devices, body(): lax.all_to_all(outgoing, 'mp', split_axis=1, concat_axis=2, tiled=True)  28.5 us
    convert_element_type x3, local copies, waits for them, and re-layouts, body(): grad_gated = returned.reshape(rows, NBLK, nlocal, 2).transpose(0, 2, 1, 3...  25 us
    reshape x3, local copies, waits for them, and re-layouts, body(): gated.reshape(rows, nlocal, NBLK, 2).transpose(0, 2, 1, 3)  13.2 us
  transfers between devices with their start and end apart: 3, of which 2 were waited for; matrix products, arithmetic and copies ran while one was open for 10% of the time, Pallas kernels for 0%

commit v1 on v0

--- a/solution.py
+++ b/solution.py
@@ -52,8 +52,23 @@
     grad_input = (
         cotangent.astype(jnp.float32) + rstd * (scaled - xf * rstd * rstd * mean_inner)
     ).astype(jnp.bfloat16)
-    left_total, gate_total, right_total = lax.psum((left_local, gate_local, right_local), "dp")
+    left_total, gate_total, right_total = dp_all_reduce((left_local, gate_local, right_local))
     return (grad_input, left_total, gate_total, right_total)
+
+
+def dp_all_reduce(parts):
+    ndp = lax.axis_size("dp")
+    shapes = [p.shape for p in parts]
+    flat = jnp.concatenate([p.reshape(-1) for p in parts]).reshape(ndp, -1)
+    mine = jnp.sum(lax.all_to_all(flat, "dp", 0, 0, tiled=True), axis=0)
+    copies = jnp.broadcast_to(mine[None], (ndp,) + mine.shape)
+    whole = lax.all_to_all(copies, "dp", 0, 0, tiled=True).reshape(-1)
+    out, at = [], 0
+    for shape in shapes:
+        size = shape[0] * shape[1] * shape[2]
+        out.append(whole[at:at + size].reshape(shape))
+        at += size
+    return tuple(out)
 
 
 def solution(mesh):

time: 505 us -> 284 us (0.56)
  the two profiles are of different devices: /device:TPU:6 before, /device:TPU:66 now
where the time goes in v1:
time: 284 us; the launch traced here: 279 us
  blocking collectives  107 us (38%)
  local copies, waits for them, and re-layouts  67.9 us (24%)
  waiting for transfers between devices  32.8 us (12%)
  matrix products  30.9 us (11%)
  other arithmetic  23.4 us (8%)
  starting transfers between devices  16.3 us (6%)
    all_to_all x1, blocking collectives, dp_all_reduce(): mine = jnp.sum(lax.all_to_all(flat, 'dp', 0, 0, tiled=True), axis=0)  45.8 us
    psum x1, blocking collectives, body(): squares = lax.psum(jnp.sum(xf * xf, axis=1), 'mp')  37.3 us
    all_to_all x1, waiting for transfers between devices, body(): lax.all_to_all(outgoing, 'mp', split_axis=1, concat_axis=2, tiled=True)  32.8 us
    convert_element_type x3, local copies, waits for them, and re-layouts, body(): grad_gated = returned.reshape(rows, NBLK, nlocal, 2).transpose(0, 2, 1, 3...  25.3 us
    psum x1, blocking collectives, body(): inner = lax.psum(jnp.sum(scaled * xf, axis=1), 'mp')  23.3 us
    reshape x3, local copies, waits for them, and re-layouts, body(): gated.reshape(rows, nlocal, NBLK, 2).transpose(0, 2, 1, 3)  13.2 us
    dot_general x1, matrix products, body(): jnp.einsum('tic,icj->tij', xn, left_blocks, preferred_element_type=jnp.fl...  9.66 us
    all_to_all x1, starting transfers between devices, dp_all_reduce(): whole = lax.all_to_all(copies, 'dp', 0, 0, tiled=True).reshape(-1)  7.01 us
  transfers between devices with their start and end apart: 3, of which 1 were waited for; matrix products, arithmetic and copies ran while one was open for 17% of the time, Pallas kernels for 0%

profile of v1, /device:TPU:66, one launch (start us, length us, event | category | flops | bytes accessed | tf_op | source)
XLA Modules:
  0.0 279.1 jit_solution(18059693909389794686)
XLA Ops:
  3.8 3.4 %copy.100 = bf16[768,16,128]{0,1,2:T(8,128)(2,1)} copy(bf16[768,16,128]{0,2,1:T(8,128)(2,1)S(1)} %convert_bitcast_fusion.1) | data formatting | bytes 6291456 | tf_op jit(solution)/shard_map/convert_element_type | solution.py:28
  7.2 4.6 %all-to-all-start = ((bf16[768,16,128]{0,1,2:T(8,128)(2,1)}), bf16[768,16,128]{0,1,2:T(8,128)(2,1)}, u32[]{:S(2)}, u32[]{:S(2)}) async-start(bf16[768,16,128]{0,1,2:T(8,128)(2,1)} %copy.100), calls=%async_computation | async-start | bytes 6291456 | tf_op jit(solution)/shard_map/all_to_all | solution.py:33
  14.4 37.3 %psum.14 = f32[768]{0:T(1024)S(1)} all-reduce(f32[768]{0:T(1024)S(1)} %fusion.8), channel_id=1, replica_groups=mesh['dp'=32,'mp'=4] {'mp'}, use_global_device_ids=true, to_apply=%region_1.0 | all-reduce | flops 768 | bytes 6144 | tf_op jit(solution)/shard_map/psum | solution.py:15
  51.8 4.3 %fusion.2 = bf16[768,2048]{1,0:T(8,128)(2,1)} fusion(bf16[768,2048]{1,0:T(8,128)(2,1)} %param.6, f32[2048]{0:T(1024)S(1)} %copy-done.6, f32[768]{0:T(1024)S(1)} %add_rsqrt_fusion), kind=kLoop, calls=%fused_computation.5 | loop fusion | flops 6291456 | bytes 6302720 | tf_op jit(solution)/shard_map/convert_element_type | solution.py:17
  56.1 4.8 %copy.127 = bf16[768,2048]{0,1:T(8,128)(2,1)} copy(bf16[768,2048]{1,0:T(8,128)(2,1)} %fusion.2) | data formatting | bytes 6291456 | tf_op jit(solution)/shard_map/reshape | solution.py:17
  61.0 5.6 %fusion.27 = f32[16,768,128]{1,2,0:T(8,128)} fusion(bf16[768,16,128]{0,2,1:T(8,128)(2,1)} %bitcast.90, bf16[16,128,128]{2,1,0:T(8,128)(2,1)S(1)} %copy-done.5), kind=kOutput, calls=%fused_computation.40 | convolution fusion | flops 402653184 | bytes 9961472 | tf_op jit(solution)/shard_map/tic,icj->tij/dot_general | solution.py:19
  70.3 6.3 %copy.102 = f32[768,4,16,32]{0,2,1,3:T(8,128)} copy(f32[768,4,16,32]{0,3,1,2:T(8,128)S(1)} %convert_bitcast_fusion) | data formatting | bytes 12582912 | tf_op jit(solution)/shard_map/convert_element_type | solution.py:38
  76.6 10.4 %copy.103 = f32[768,16,64,2]{0,3,2,1:T(2,128)} copy(f32[768,16,64,2]{0,2,3,1:T(8,128)} %bitcast.94) | data formatting | bytes 12582912 | tf_op jit(solution)/shard_map/convert_element_type | solution.py:38
  86.9 8.7 %reshape.71 = f32[768,16,128]{0,2,1:T(8,128)} reshape(f32[768,16,64,2]{0,3,2,1:T(2,128)} %copy.103) | data formatting | bytes 12582912 | tf_op jit(solution)/shard_map/convert_element_type | solution.py:38
  95.6 9.7 %fusion.13 = (bf16[768,16,128]{0,2,1:T(8,128)(2,1)}, bf16[768,16,128]{0,2,1:T(8,128)(2,1)}, bf16[768,16,128]{0,2,1:T(8,128)(2,1)}) fusion(f32[16,768,128]{1,2,0:T(8,128)} %fusion.27, f32[768,16,128]{0,2,1:T(8,128)} %reshape.71, bf16[768,16,128]{0,2,1:T(8,128)(2,1)} %bitcast.91, bf16[16,128,128]{2,1,0:T(8,128)(2,1)S(1)} %copy-done), kind=kOutput, calls=%fused_computation.19 | convolution fusion | flops 426246144 | bytes 25690112 | tf_op jit(solution)/shard_map/tic,icj->tij/dot_general | solution.py:18
  105.3 7.3 %reshape.68 = bf16[768,16,64,2]{0,3,2,1:T(2,128)(2,1)} reshape(bf16[768,16,128]{0,2,1:T(8,128)(2,1)} %get-tuple-element.4) | data formatting | bytes 6291456 | tf_op jit(solution)/shard_map/reshape | solution.py:23
  118.5 4.7 %all-to-all-start.1 = ((bf16[768,64,32]{0,2,1:T(8,128)(2,1)}), bf16[768,64,32]{0,2,1:T(8,128)(2,1)}, u32[]{:S(2)}, u32[]{:S(2)}) async-start(bf16[768,64,32]{0,2,1:T(8,128)(2,1)} %copy.116), calls=%async_computation.1 | async-start | bytes 6291456 | tf_op jit(solution)/shard_map/all_to_all | solution.py:29
  123.2 4.0 %fusion.29 = f32[16,128,128]{2,1,0:T(8,128)S(1)} fusion(bf16[768,16,128]{0,2,1:T(8,128)(2,1)} %bitcast.92, bf16[768,16,128]{0,2,1:T(8,128)(2,1)} %get-tuple-element.5), kind=kOutput, calls=%fused_computation.42 | convolution fusion | flops 402653184 | bytes 7340032 | tf_op jit(solution)/shard_map/tic,tij->icj/dot_general | solution.py:44
  128.9 32.8 %all-to-all-done.1 = bf16[768,64,32]{0,2,1:T(8,128)(2,1)} async-done(((bf16[768,64,32]{0,2,1:T(8,128)(2,1)}), bf16[768,64,32]{0,2,1:T(8,128)(2,1)}, u32[]{:S(2)}, u32[]{:S(2)}) %all-to-all-start.1) | async-done | bytes 3145760 | tf_op jit(solution)/shard_map/all_to_all | solution.py:29
  165.7 45.8 %all_to_all.45 = f32[32,1,24576]{2,1,0:T(1,128)} all-to-all(f32[32,1,24576]{2,1,0:T(1,128)S(1)} %bitcast.96), channel_id=1, replica_groups=mesh['dp'=32,'mp'=4] {'dp'}, dimensions={0} | all-to-all | bytes 6291456 | tf_op jit(solution)/shard_map/all_to_all | solution.py:63
  211.6 3.9 %reduce_sum.29 = f32[24576]{0:T(1024)S(1)} reduce(f32[32,1,24576]{2,1,0:T(1,128)} %all_to_all.45, f32[]{:T(128)} %constant.4.clone.1), dimensions={0,1}, to_apply=%region_4.5 | reduce | flops 761856 | bytes 3244036 | tf_op jit(solution)/shard_map/reduce_sum | solution.py:63
  215.5 4.5 %broadcast_in_dim.2 = f32[32,1,24576]{2,1,0:T(1,128)} broadcast(f32[24576]{0:T(1024)S(1)} %reduce_sum.29), dimensions={2} | broadcast | bytes 3244032 | tf_op jit(solution)/shard_map/broadcast_in_dim | solution.py:64
  220.0 7.0 %all-to-all-start.3 = ((f32[32,1,24576]{2,1,0:T(1,128)}), f32[32,1,24576]{2,1,0:T(1,128)}, u32[]{:S(2)}, u32[]{:S(2)}) async-start(f32[32,1,24576]{2,1,0:T(1,128)} %broadcast_in_dim.2), calls=%async_computation.3 | async-start | bytes 6291456 | tf_op jit(solution)/shard_map/all_to_all | solution.py:65
  230.0 3.6 %convolution_add_fusion = f32[16,768,128]{1,2,0:T(8,128)} fusion(f32[16,768,128]{1,2,0:T(8,128)S(1)} %fusion.30, bf16[16,128,128]{2,1,0:T(8,128)(2,1)S(1)} %copy-done.5, bf16[768,16,128]{0,2,1:T(8,128)(2,1)S(1)} %copy-done.4), kind=kOutput, calls=%fused_computation.36 | convolution fusion | flops 404226048 | bytes 16252928 | tf_op jit(solution)/shard_map/tij,icj->tic/dot_general | solution.py:46
  233.6 6.6 %copy.110 = f32[768,2048]{1,0:T(8,128)} copy(f32[768,2048]{0,1:T(8,128)} %bitcast.95) | data formatting | bytes 12582912 | tf_op jit(solution)/shard_map/reshape | solution.py:49
  240.2 4.6 %fusion.9 = f32[768]{0:T(1024)S(1)} fusion(bf16[768,2048]{1,0:T(8,128)(2,1)} %param.6, f32[768,2048]{1,0:T(8,128)} %copy.110, f32[2048]{0:T(1024)S(1)} %copy-done.6), kind=kLoop, calls=%fused_computation.12 | loop fusion | flops 6290688 | bytes 9448448 | tf_op jit(solution)/shard_map/reduce_sum | solution.py:50
  244.8 23.3 %psum.15 = f32[768]{0:T(1024)S(1)} all-reduce(f32[768]{0:T(1024)S(1)} %fusion.9), channel_id=1, replica_groups=mesh['dp'=32,'mp'=4] {'mp'}, use_global_device_ids=true, to_apply=%region_3.4 | all-reduce | flops 768 | bytes 6144 | tf_op jit(solution)/shard_map/psum | solution.py:50
  268.2 6.9 %fusion.7 = bf16[768,2048]{1,0:T(8,128)(2,1)} fusion(bf16[768,2048]{1,0:T(8,128)(2,1)} %param.6, bf16[768,2048]{1,0:T(8,128)(2,1)} %param.11, f32[768,2048]{1,0:T(8,128)} %copy.110, f32[768]{0:T(1024)S(1)} %broadcast_multiply_fusion, f32[2048]{0:T(1024)S(1)} %copy-done.6, f32[768]{0:T(1024)S(1)} %add_rsqrt_fusion), kind=kLoop, calls=%fused_computation.10 | loop fusion | flops 15728640 | bytes 15742976 | tf_op jit(solution)/shard_map/convert_element_type | solution.py:54
  275.1 3.6 %fusion.26 = (f32[16,128,128]{2,1,0:T(8,128)}, f32[16,128,128]{2,1,0:T(8,128)}, f32[16,128,128]{2,1,0:T(8,128)}) fusion(f32[48,128,128]{2,1,0:T(8,128)} %bitcast.18), kind=kLoop, calls=%fused_computation.39 | loop fusion | bytes 6291456 | tf_op jit(solution)/shard_map/slice | solution.py:69
  (29 shorter events, 24.1 us)
Async XLA Ops:
  0.6 95.0 %copy-start = (bf16[16,128,128]{2,1,0:T(8,128)(2,1)S(1)}, bf16[16,128,128]{2,1,0:T(8,128)(2,1)}, u32[]{:S(2)}) copy-start(bf16[16,128,128]{2,1,0:T(8,128)(2,1)} %param.8) | copy-start | bytes 1572868
  7.2 59.4 %all-to-all-start = ((bf16[768,16,128]{0,1,2:T(8,128)(2,1)}), bf16[768,16,128]{0,1,2:T(8,128)(2,1)}, u32[]{:S(2)}, u32[]{:S(2)}) async-start(bf16[768,16,128]{0,1,2:T(8,128)(2,1)} %copy.100), calls=%async_computation | async-start | bytes 6291456 | tf_op jit(solution)/shard_map/all_to_all | solution.py:33
  11.8 39.9 %copy-start.6 = (f32[2048]{0:T(1024)S(1)}, f32[2048]{0:T(1024)}, u32[]{:S(2)}) copy-start(f32[2048]{0:T(1024)} %param.7) | copy-start | bytes 24580
  56.1 4.8 %copy-start.5 = (bf16[16,128,128]{2,1,0:T(8,128)(2,1)S(1)}, bf16[16,128,128]{2,1,0:T(8,128)(2,1)}, u32[]{:S(2)}) copy-start(bf16[16,128,128]{2,1,0:T(8,128)(2,1)} %param.9) | copy-start | bytes 1572868
  118.5 43.2 %all-to-all-start.1 = ((bf16[768,64,32]{0,2,1:T(8,128)(2,1)}), bf16[768,64,32]{0,2,1:T(8,128)(2,1)}, u32[]{:S(2)}, u32[]{:S(2)}) async-start(bf16[768,64,32]{0,2,1:T(8,128)(2,1)} %copy.116), calls=%async_computation.1 | async-start | bytes 6291456 | tf_op jit(solution)/shard_map/all_to_all | solution.py:29
  123.2 4.0 %copy-start.1 = (bf16[768,2048]{0,1:T(8,128)(2,1)S(1)}, bf16[768,2048]{0,1:T(8,128)(2,1)}, u32[]{:S(2)}) copy-start(bf16[768,2048]{0,1:T(8,128)(2,1)} %copy.127) | copy-start | bytes 9437188
  123.2 4.7 %copy-start.2 = (bf16[768,16,128]{0,2,1:T(8,128)(2,1)S(1)}, bf16[768,16,128]{0,2,1:T(8,128)(2,1)}, u32[]{:S(2)}) copy-start(bf16[768,16,128]{0,2,1:T(8,128)(2,1)} %get-tuple-element.6) | copy-start | bytes 9437188
  161.7 2.8 %copy-start.3 = (bf16[768,2048]{1,0:T(8,128)(2,1)S(1)}, bf16[768,2048]{1,0:T(8,128)(2,1)}, u32[]{:S(2)}) copy-start(bf16[768,2048]{1,0:T(8,128)(2,1)} %param.11) | copy-start | bytes 9437188
  220.0 55.1 %all-to-all-start.3 = ((f32[32,1,24576]{2,1,0:T(1,128)}), f32[32,1,24576]{2,1,0:T(1,128)}, u32[]{:S(2)}, u32[]{:S(2)}) async-start(f32[32,1,24576]{2,1,0:T(1,128)} %broadcast_in_dim.2), calls=%async_computation.3 | async-start | bytes 6291456 | tf_op jit(solution)/shard_map/all_to_all | solution.py:65
  227.0 3.0 %copy-start.4 = (bf16[768,16,128]{0,2,1:T(8,128)(2,1)S(1)}, bf16[768,16,128]{0,2,1:T(8,128)(2,1)}, u32[]{:S(2)}) copy-start(bf16[768,16,128]{0,2,1:T(8,128)(2,1)} %get-tuple-element.5) | copy-start | bytes 9437188
